TPU v7x, 256 devices: a whole 4x4x8 slice. The times are simulated.
256 devices in a mesh: req: 64 (over x, y_lo, z), tp: 4 (over y_hi, core).
Axes of the slice: x: 4, y: 4 (y_hi: 2, y_lo: 2; y = y_hi * 2 + y_lo), z: 8, core: 2. Of those that a mesh axis runs over, the one named last changes fastest.
Arguments:
- hidden_in: bfloat16 [8192, 2048], P('req')
- attn_gain: float32 [2048], replicated, may hold values from 0.1 to 1.9
- w_query: bfloat16 [2048, 2048], P(None, 'tp'), may hold values from -0.125 to 0.125
- w_keyval: bfloat16 [2048, 4, 256], P(None, 'tp'), may hold values from -0.125 to 0.125
- w_out: bfloat16 [2048, 2048], P('tp'), may hold values from -0.125 to 0.125
- moe_gain: float32 [2048], replicated, may hold values from 0.1 to 1.9
- w_gate_up: bfloat16 [64, 2, 2048, 1408], P('req', None, None, 'tp'), may hold values from -0.125 to 0.125
- w_down: bfloat16 [64, 1408, 2048], P('req', 'tp'), may hold values from -0.15625 to 0.15625
- seg_ids: int32 [64, 128], P('req'), may hold values from 0 to 3, never falling along the last dimension, each value on 1 to 64 neighbouring positions
- cached_len: int32 [64], P('req'), may hold values from 2048 to 4096, as said below
- page_table: int32 [64, 32], P('req'), may hold values from 0 to 1023, as said below
- cache_pool: bfloat16 [1024, 4, 128, 256], P('req', 'tp')
- expert_ids: int32 [8192, 6], P('req'), may hold values from 0 to 63, all different within a row; in each aligned block of 128 rows (0 to 127, 128 to 255, ...) at most 16 rows name the same one
- expert_weights: float32 [8192, 6], P('req'), may hold values from 0.05 to 0.5
Outputs:
- layer_out: bfloat16 [8192, 2048], P('req')
Inputs may be any that keep to these rules, and one draw needn't show every extreme that they name: `seg_ids`: row r holds the prompt numbers of pack r, never falling along the row; each prompt has 1 to 64 tokens, one exactly that many. `cached_len`: some pack has exactly 4096 cached tokens. `page_table`: entry j of row r names the page holding tokens j * 128 to (j + 1) * 128 - 1 of pack r's cached prefix; page p lies on index p // 16 of req. At most 1 entries of one row lie on one owner, and in every row some owner holds exactly 1. Entries past the cached length name pages too. `expert_ids`: each row names 6 different experts. Among the rows of one pack no expert is named more than 16 times, a bound that some block reaches.
All inputs are finite; a program needn't handle non-finite values.
Results may differ from a plain program's by a relative error of at most 0.009.
Values may be sent and summed in bfloat16 or wider, within the bound.
No kernel may reach another device: no remote copies, remote signals or barrier semaphores. Data moves between devices by JAX's collectives and lax.ppermute only.
A program may use at most 128 MiB of HBM per device.

v0:
```python
import math
import jax
import jax.numpy as jnp
from jax import lax
from jax.sharding import PartitionSpec as P

eps = 1e-06
rope_base = 600000.0


def rms_scale(rows_in, gain):
    widened = rows_in.astype(jnp.float32)
    return widened * lax.rsqrt(jnp.mean(widened * widened, axis=-1, keepdims=True) + eps) * gain


def rotate(vectors, angles):
    half_dim = vectors.shape[-1] // 2
    first_half = vectors[..., :half_dim]
    second_half = vectors[..., half_dim:]
    cosine = jnp.cos(angles)[:, None, :]
    sine_vals = jnp.sin(angles)[:, None, :]
    return jnp.concatenate(
        [
            first_half * cosine - second_half * sine_vals,
            second_half * cosine + first_half * sine_vals,
        ],
        axis=-1,
    )


def positions(segment_row, cached):
    length = segment_row.shape[0]
    token_index = jnp.arange(length, dtype=jnp.int32)
    begins = jnp.concatenate([jnp.ones((1,), dtype=bool), segment_row[1:] != segment_row[:-1]])
    seg_start = lax.cummax(jnp.where(begins, token_index, 0), axis=0)
    carried = segment_row == segment_row[0]
    place = token_index - seg_start + jnp.where(carried, cached, 0)
    return (place, carried)


def make_angles(place, head_dim):
    inverse = rope_base ** (-(jnp.arange(head_dim // 2, dtype=jnp.float32) * 2.0 / head_dim))
    return place.astype(jnp.float32)[:, None] * inverse[None, :]


def admit(segment_row, carried, cached, prefix_len):
    length = segment_row.shape[0]
    token_index = jnp.arange(length, dtype=jnp.int32)
    prefix_ok = (jnp.arange(prefix_len, dtype=jnp.int32)[None, :] < cached) & carried[:, None]
    local_ok = (segment_row[:, None] == segment_row[None, :]) & (
        token_index[None, :] <= token_index[:, None]
    )
    return jnp.concatenate([prefix_ok, local_ok], axis=1)


def attend(queries, all_keys, all_values, admitted):
    scale = 1.0 / math.sqrt(queries.shape[-1])
    scores = (
        jnp.einsum("tkgd,knd->kgtn", queries, all_keys, preferred_element_type=jnp.float32) * scale
    )
    scores = jnp.where(admitted[None, None], scores, -1e30)
    highest = jnp.max(scores, axis=-1, keepdims=True)
    expo = jnp.exp(scores - highest)
    totals = jnp.sum(expo, axis=-1, keepdims=True)
    weights = (expo / totals).astype(jnp.bfloat16)
    context = jnp.einsum("kgtn,knd->tkgd", weights, all_values, preferred_element_type=jnp.float32)
    return context.astype(jnp.bfloat16)


def shards(
    hidden_in,
    attn_gain,
    w_query,
    w_keyval,
    w_out,
    moe_gain,
    w_gate_up,
    w_down,
    seg_ids,
    cached_len,
    page_table,
    cache_pool,
    expert_ids,
    expert_weights,
):
    tok_rows, model_width = hidden_in.shape
    head_dim = w_keyval.shape[2] // 2
    kv_local = w_keyval.shape[1]
    q_local = w_query.shape[1] // head_dim
    group_size = q_local // kv_local
    segment_row = seg_ids[0]
    cached = cached_len[0]
    place, carried = positions(segment_row, cached)
    angles = make_angles(place, head_dim)
    normed = rms_scale(hidden_in, attn_gain).astype(jnp.bfloat16)
    n_req = lax.axis_size("req")
    listed = page_table[0]
    pref_pages = listed.shape[0]
    pages_dev = cache_pool.shape[0]
    page_len = cache_pool.shape[2]
    cap_pages = (2 * pref_pages + n_req - 1) // n_req
    owners = listed // pages_dev
    entry_index = jnp.arange(pref_pages, dtype=jnp.int32)
    earlier = (owners[None, :] == owners[:, None]) & (entry_index[None, :] < entry_index[:, None])
    owner_rank = jnp.sum(earlier.astype(jnp.int32), axis=1)
    page_slot = listed % pages_dev
    cap_index = jnp.arange(cap_pages, dtype=jnp.int32)
    owner_index = jnp.arange(n_req, dtype=jnp.int32)
    wanted = (owners[None, None, :] == owner_index[:, None, None]) & (
        owner_rank[None, None, :] == cap_index[None, :, None]
    )
    request = jnp.sum(jnp.where(wanted, page_slot[None, None, :], 0), axis=2)
    asked_slots = lax.all_to_all(request, "req", split_axis=0, concat_axis=0, tiled=True)
    served = cache_pool[asked_slots.reshape(-1)].reshape(
        n_req, cap_pages, kv_local, page_len, 2 * head_dim
    )
    fetched = lax.all_to_all(served, "req", split_axis=0, concat_axis=0, tiled=True)
    fetched = fetched.reshape(n_req * cap_pages, kv_local, page_len, 2 * head_dim)[
        owners * cap_pages + owner_rank
    ]
    prefix = jnp.transpose(fetched, (1, 0, 2, 3)).reshape(
        kv_local, pref_pages * page_len, 2 * head_dim
    )
    queries = jnp.dot(normed, w_query, preferred_element_type=jnp.float32).reshape(
        tok_rows, q_local, head_dim
    )
    queries = (
        rotate(queries, angles)
        .astype(jnp.bfloat16)
        .reshape(tok_rows, kv_local, group_size, head_dim)
    )
    keyval = jnp.dot(
        normed,
        w_keyval.reshape(model_width, kv_local * 2 * head_dim),
        preferred_element_type=jnp.float32,
    ).reshape(tok_rows, kv_local, 2 * head_dim)
    keys_new = rotate(keyval[..., :head_dim], angles).astype(jnp.bfloat16)
    values_new = keyval[..., head_dim:].astype(jnp.bfloat16)
    all_keys = jnp.concatenate([prefix[..., :head_dim], jnp.transpose(keys_new, (1, 0, 2))], axis=1)
    all_values = jnp.concatenate(
        [prefix[..., head_dim:], jnp.transpose(values_new, (1, 0, 2))], axis=1
    )
    admitted = admit(segment_row, carried, cached, pref_pages * page_len)
    context = attend(queries, all_keys, all_values, admitted).reshape(tok_rows, q_local * head_dim)
    attention = lax.psum(jnp.dot(context, w_out, preferred_element_type=jnp.float32), "tp")
    resid = (hidden_in.astype(jnp.float32) + attention).astype(jnp.bfloat16)
    moe_in = rms_scale(resid, moe_gain).astype(jnp.bfloat16)
    topk = expert_ids.shape[1]
    n_exp = n_req * w_gate_up.shape[0]
    cap_e = 4 * tok_rows * topk // (3 * n_exp)
    flat_ids = expert_ids.reshape(-1)
    onehot = (flat_ids[:, None] == jnp.arange(n_exp, dtype=jnp.int32)[None, :]).astype(jnp.int32)
    slot_rank = jnp.sum((jnp.cumsum(onehot, axis=0) - 1) * onehot, axis=1)
    assign_slot = flat_ids * cap_e + slot_rank
    slot_match = assign_slot[None, :] == jnp.arange(n_exp * cap_e, dtype=jnp.int32)[:, None]
    selector = jnp.any(slot_match.reshape(n_exp * cap_e, tok_rows, topk), axis=2).astype(
        jnp.bfloat16
    )
    n_tp = lax.axis_size("tp")
    tp_me = lax.axis_index("tp")
    cap_q = cap_e // n_tp
    sel_q = lax.dynamic_slice_in_dim(
        selector.reshape(n_exp, cap_e, tok_rows), tp_me * cap_q, cap_q, axis=1
    )
    outgoing = (
        jnp.einsum("ecs,sd->ecd", sel_q, moe_in, preferred_element_type=jnp.float32)
        .astype(jnp.bfloat16)
        .reshape(n_exp, cap_q * model_width)
    )
    expert_q = lax.all_to_all(outgoing, "req", split_axis=0, concat_axis=0, tiled=True)
    expert_in = lax.all_gather(expert_q, "tp", axis=1, tiled=True)
    expert_rows = expert_in.reshape(-1, model_width)
    gate_part = jnp.dot(expert_rows, w_gate_up[0, 0], preferred_element_type=jnp.float32)
    up_part = jnp.dot(expert_rows, w_gate_up[0, 1], preferred_element_type=jnp.float32)
    hidden_act = (jax.nn.silu(gate_part) * up_part).astype(jnp.bfloat16)
    partial = (
        jnp.dot(hidden_act, w_down[0], preferred_element_type=jnp.float32)
        .astype(jnp.bfloat16)
        .reshape(n_req, cap_e * model_width)
    )
    expert_share = lax.psum_scatter(partial, "tp", scatter_dimension=1, tiled=True)
    results_q = lax.all_to_all(expert_share, "req", split_axis=0, concat_axis=0, tiled=True)
    results = lax.all_gather(results_q, "tp", axis=1, tiled=True)
    picked = results.reshape(-1, model_width)[assign_slot].reshape(tok_rows, topk, model_width)
    moe_out = jnp.sum(expert_weights[:, :, None] * picked.astype(jnp.float32), axis=1)
    return (resid.astype(jnp.float32) + moe_out).astype(jnp.bfloat16)


def solution(mesh):
    in_specs = (
        P("req", None),
        P(),
        P(None, "tp"),
        P(None, "tp", None),
        P("tp", None),
        P(),
        P("req", None, None, "tp"),
        P("req", "tp", None),
        P("req", None),
        P("req"),
        P("req", None),
        P("req", "tp", None, None),
        P("req", None),
        P("req", None),
    )
    out_specs = P("req", None)
    return jax.shard_map(shards, mesh=mesh, in_specs=in_specs, out_specs=out_specs, check_vma=False)
```

profile of v0, /device:TPU:1, one launch (start us, length us, event | category | flops | bytes accessed | tf_op | source)
XLA Modules:
  0.0 605.5 jit_solution(16908138329106039818)
XLA Ops:
  8.4 22.6 %all_to_all.42 = s32[64,1,1]{2,1,0:T(1,128)S(1)} all-to-all(s32[64,1,1]{2,1,0:T(1,128)S(1)} %copy.63), channel_id=1, replica_groups=mesh['req'=64,'tp'=4] {'req'}, dimensions={0} | all-to-all | bytes 512 | tf_op jit(solution)/shard_map/all_to_all | solution.py:113
  32.2 4.0 gather_fusion
  36.2 5.8 all-to-all-start.1
  43.5 2.1 fusion.41
  48.4 2.1 broadcast_and_fusion
  50.6 82.7 %all-to-all-done.1 = bf16[64,1,1,128,256]{4,3,2,1,0:T(8,128)(2,1)} async-done(((bf16[64,1,1,128,256]{4,3,2,1,0:T(8,128)(2,1)}), bf16[64,1,1,128,256]{4,3,2,1,0:T(8,128)(2,1)}, u32[]{:S(2)}, u32[]{:S(2)}) %all-to-all-start.1) | async-done | bytes 4194336 | tf_op jit(solution)/shard_map/all_to_all | solution.py:117
  133.3 4.2 gather_fusion.1
  141.7 1.7 fusion.13
  145.9 1.8 reduce-window.19
  149.0 48.8 %all-reduce.2.cloned.1.call-done = f32[128,2048]{1,0:T(8,128)} async-done(((f32[128,2048]{1,0:T(8,128)}), f32[128,2048]{1,0:T(8,128)}) %all-reduce.2.cloned.1.call-update) | async-done | bytes 1048592 | tf_op jit(solution)/shard_map/psum | solution.py:145
  199.8 1.8 copy.76
  201.6 6.2 %all_to_all.37 = bf16[64,1,8192]{2,1,0:T(2,128)(2,1)S(1)} reshape(bf16[64,4,2048]{2,1,0:T(4,128)(2,1)} %copy.76) | data formatting | bytes 2097152 | tf_op jit(solution)/shard_map/all_to_all | solution.py:170
  208.3 8.1 %reduce.11 = bf16[64,8192]{1,0:T(8,128)(2,1)} reduce(bf16[64,1,8192]{2,1,0:T(2,128)(2,1)S(1)} %all_to_all.37, bf16[]{:T(256)} %broadcast.486), dimensions={1}, to_apply=%all_to_all.37.reduce_sub_computation | reduce | bytes 2097154 | tf_op jit(solution)/shard_map/all_to_all | solution.py:170
  216.5 1.8 reshape.700
  218.3 36.8 %all_to_all.43 = bf16[64,2,4096]{2,1,0:T(2,128)(2,1)S(1)} all-to-all(bf16[64,2,4096]{2,1,0:T(2,128)(2,1)S(1)} %reshape.700), channel_id=1, replica_groups=mesh['req'=64,'tp'=4] {'req'}, dimensions={0} | all-to-all | bytes 2097152 | tf_op jit(solution)/shard_map/all_to_all | solution.py:170
  255.1 3.5 reshape.701
  258.9 63.4 %all-gather.5.cloned.1.call-done = bf16[64,1,32768]{2,1,0:T(2,128)(2,1)} async-done(((bf16[64,1,8192]{2,1,0:T(2,128)(2,1)}), bf16[64,1,32768]{2,1,0:T(2,128)(2,1)}) %all-gather.5.cloned.1.call-update) | async-done | bytes 4194320 | tf_op jit(solution)/shard_map/all_gather | solution.py:171
  322.3 26.1 %reduce.6 = bf16[64,32768]{1,0:T(8,128)(2,1)} reduce(bf16[64,1,32768]{2,1,0:T(2,128)(2,1)} %all-gather.5.cloned.1.call-done, bf16[]{:T(256)} %constant.92), dimensions={1}, to_apply=%all-gather.reduce_sub_computation | reduce | bytes 8388610 | tf_op jit(solution)/shard_map/all_gather | solution.py:171
  348.4 7.4 %reshape.652 = bf16[1024,2048]{1,0:T(8,128)(2,1)} reshape(bf16[64,32768]{1,0:T(8,128)(2,1)} %reduce.6) | data formatting | bytes 8388608 | tf_op jit(solution)/shard_map/reshape | solution.py:172
  355.8 5.6 fusion.6
  361.4 9.0 %convolution_convert_fusion = bf16[1024,2048]{1,0:T(8,128)(2,1)} fusion(bf16[1,352,2048]{2,1,0:T(8,128)(2,1)S(1)} %copy-done.8, bf16[1024,2048]{1,0:T(8,128)(2,1)} %reshape.652, bf16[1,2,2048,352]{2,3,1,0:T(8,128)(2,1)} %param.20, f32[1024,352]{0,1:T(8,128)} %fusion.6), kind=kOutput, calls=%fused_computation.10 | convolution fusion | flops 2957049856 | bytes 12713984 | tf_op jit(solution)/shard_map/dot_general | solution.py:177
  370.4 7.4 %reshape.653 = bf16[64,32768]{1,0:T(8,128)(2,1)} reshape(bf16[1024,2048]{1,0:T(8,128)(2,1)} %convolution_convert_fusion) | data formatting | bytes 8388608 | tf_op jit(solution)/shard_map/reshape | solution.py:179
  377.9 55.6 %reduce-scatter.2.cloned.1.call-done = bf16[64,8192]{1,0:T(8,128)(2,1)} async-done(((bf16[64,32768]{1,0:T(8,128)(2,1)}), bf16[64,8192]{1,0:T(8,128)(2,1)}) %reduce-scatter.2.cloned.1.call-update) | async-done | bytes 1048592 | tf_op jit(solution)/shard_map/reduce_scatter | solution.py:181
  433.5 2.7 reduce.12
  436.9 36.9 %all_to_all.44 = bf16[64,2,4096]{2,1,0:T(2,128)(2,1)S(1)} all-to-all(bf16[64,2,4096]{2,1,0:T(2,128)(2,1)S(1)} %reshape.702), channel_id=1, replica_groups=mesh['req'=64,'tp'=4] {'req'}, dimensions={0} | all-to-all | bytes 2097152 | tf_op jit(solution)/shard_map/all_to_all | solution.py:182
  473.8 3.5 reshape.703
  477.7 63.5 %all-gather.7.cloned.1.call-done = bf16[64,1,32768]{2,1,0:T(2,128)(2,1)} async-done(((bf16[64,1,8192]{2,1,0:T(2,128)(2,1)}), bf16[64,1,32768]{2,1,0:T(2,128)(2,1)}) %all-gather.7.cloned.1.call-update) | async-done | bytes 4194320 | tf_op jit(solution)/shard_map/all_gather | solution.py:183
  541.2 26.1 %reduce.7 = bf16[64,32768]{1,0:T(8,128)(2,1)} reduce(bf16[64,1,32768]{2,1,0:T(2,128)(2,1)} %all-gather.7.cloned.1.call-done, bf16[]{:T(256)} %constant.92), dimensions={1}, to_apply=%all-gather.1.reduce_sub_computation | reduce | bytes 8388610 | tf_op jit(solution)/shard_map/all_gather | solution.py:183
  567.3 7.4 %reshape.654 = bf16[1024,2048]{1,0:T(8,128)(2,1)} reshape(bf16[64,32768]{1,0:T(8,128)(2,1)} %reduce.7) | data formatting | bytes 8388608 | tf_op jit(solution)/shard_map/reshape | solution.py:184
  574.7 9.8 %gather_fusion.2 = bf16[768,2048]{1,0:T(8,128)(2,1)} fusion(bf16[1024,2048]{1,0:T(8,128)(2,1)} %reshape.654, s32[1024]{0:T(1024)S(1)} %pad_clamp_fusion), kind=kCustom, calls=%fused_computation.2 | custom fusion | bytes 6294528 | tf_op jit(solution)/shard_map/gather | solution.py:184
  584.5 6.6 %reshape.655 = f32[128,6,2048]{2,1,0:T(8,128)} reshape(bf16[768,2048]{1,0:T(8,128)(2,1)} %gather_fusion.2) | data formatting | bytes 9437184 | tf_op jit(solution)/shard_map/convert_element_type | solution.py:185
  591.0 6.8 %multiply_reduce_fusion = f32[128,2048]{1,0:T(8,128)S(1)} fusion(f32[128,6,2048]{2,1,0:T(8,128)} %reshape.655, f32[128,6]{1,0:T(8,128)S(1)} %copy.69), kind=kLoop, calls=%fused_computation.6 | loop fusion | flops 2883584 | bytes 7343104 | tf_op jit(solution)/shard_map/reduce_sum | solution.py:185
  (84 shorter events, 19.3 us)
Async XLA Ops:
  6.5 136.9 %copy-start = (bf16[512,2048]{1,0:T(8,128)(2,1)S(1)}, bf16[512,2048]{1,0:T(8,128)(2,1)}, u32[]{:S(2)}) copy-start(bf16[512,2048]{1,0:T(8,128)(2,1)} %param.18) | copy-start | bytes 6291460
  36.2 6.5 %copy-start.5 = (s32[1,128]{1,0:T(1,128)S(1)}, s32[1,128]{1,0:T(1,128)}, u32[]{:S(2)}) copy-start(s32[1,128]{1,0:T(1,128)} %param.22) | copy-start | bytes 1540
  36.2 7.1 %copy-start.2 = (bf16[128,2048]{1,0:T(8,128)(2,1)S(1)}, bf16[128,2048]{1,0:T(8,128)(2,1)}, u32[]{:S(2)}) copy-start(bf16[128,2048]{1,0:T(8,128)(2,1)} %param.14) | copy-start | bytes 1572868
  36.2 7.3 %copy-start.3 = (f32[2048]{0:T(1024)S(1)}, f32[2048]{0:T(1024)}, u32[]{:S(2)}) copy-start(f32[2048]{0:T(1024)} %param.15) | copy-start | bytes 24580
  36.2 97.1 %all-to-all-start.1 = ((bf16[64,1,1,128,256]{4,3,2,1,0:T(8,128)(2,1)}), bf16[64,1,1,128,256]{4,3,2,1,0:T(8,128)(2,1)}, u32[]{:S(2)}, u32[]{:S(2)}) async-start(bf16[64,1,1,128,256]{4,3,2,1,0:T(8,128)(2,1)} %bitcast.127), calls=%async_computation.1 | async-start | bytes 8388608 | tf_op jit(solution)/shard_map/all_to_all | solution.py:117
  42.0 3.7 copy-start.9
  42.0 155.8 %all-reduce.2.cloned.1.call-start = ((), (), s32[]{:S(2)}) async-start(), calls=%async_computation.5 | async-start | bytes 2097152 | tf_op jit(solution)/shard_map/psum | solution.py:145
  143.4 2.1 copy-start.6
  144.9 54.3 %copy-start.4 = (f32[2048]{0:T(1024)S(1)}, f32[2048]{0:T(1024)}, u32[]{:S(2)}) copy-start(f32[2048]{0:T(1024)} %param.19) | copy-start | bytes 24580
  145.0 177.3 %all-gather.5.cloned.1.call-start = ((), (), s32[]{:S(2)}) async-start(), calls=%async_computation.7 | async-start | bytes 10485760 | tf_op jit(solution)/shard_map/all_gather | solution.py:171
  258.7 174.8 %reduce-scatter.2.cloned.1.call-start = ((), (), s32[]{:S(2)}) async-start(), calls=%async_computation.6 | async-start | bytes 5242880 | tf_op jit(solution)/shard_map/reduce_scatter | solution.py:181
  355.8 5.6 copy-start.8
  377.8 163.3 %all-gather.7.cloned.1.call-start = ((), (), s32[]{:S(2)}) async-start(), calls=%async_computation.8 | async-start | bytes 10485760 | tf_op jit(solution)/shard_map/all_gather | solution.py:183
  473.8 3.5 copy-start.7
  591.0 7.7 %copy-start.1 = (bf16[512,2048]{1,0:T(8,128)(2,1)S(1)}, bf16[512,2048]{1,0:T(8,128)(2,1)}, u32[]{:S(2)}) copy-start(bf16[512,2048]{1,0:T(8,128)(2,1)} %param.18) | copy-start | bytes 6291460
Sparse Core Ops, SparseCore 0:
  145.1 52.6 all-reduce.1
  258.8 63.4 all-gather.4
  377.9 55.4 reduce-scatter.1
  477.5 63.6 all-gather.6
where the time goes:
time: 615 us; the launch traced here: 605 us
  waiting for transfers between devices  314 us (51%)
  blocking collectives  96.3 us (16%)
  other arithmetic  82.4 us (13%)
  local copies, waits for them, and re-layouts  68.3 us (11%)
  matrix products  23.4 us (4%)
  between operations  14.4 us (2%)
  starting transfers between devices  6.6 us (1%)
    all_to_all x1, waiting for transfers between devices, shards(): lax.all_to_all(served, 'req', split_axis=0, concat_axis=0, tiled=True)  82.7 us
    all_gather x1, waiting for transfers between devices, shards(): results = lax.all_gather(results_q, 'tp', axis=1, tiled=True)  63.5 us
    all_gather x1, waiting for transfers between devices, shards(): expert_in = lax.all_gather(expert_q, 'tp', axis=1, tiled=True)  63.4 us
    reduce_scatter x1, waiting for transfers between devices, shards(): lax.psum_scatter(partial, 'tp', scatter_dimension=1, tiled=True)  55.6 us
    psum x1, waiting for transfers between devices, shards(): lax.psum(jnp.dot(context, w_out, preferred_element_type=jnp.float32), 'tp')  48.8 us
    all_to_all x1, blocking collectives, shards(): lax.all_to_all(expert_share, 'req', split_axis=0, concat_axis=0, tiled=True)  36.9 us
    all_to_all x1, blocking collectives, shards(): lax.all_to_all(outgoing, 'req', split_axis=0, concat_axis=0, tiled=True)  36.8 us
    all_gather x1, other arithmetic, shards(): results = lax.all_gather(results_q, 'tp', axis=1, tiled=True)  26.1 us
  transfers between devices with their start and end apart: 5, of which 5 were waited for; matrix products, arithmetic and copies ran while one was open for 2% of the time, Pallas kernels for 0%

commit v1 on v0

--- a/solution.py
+++ b/solution.py
@@ -180,7 +180,9 @@
     )
     expert_share = lax.psum_scatter(partial, "tp", scatter_dimension=1, tiled=True)
     results_q = lax.all_to_all(expert_share, "req", split_axis=0, concat_axis=0, tiled=True)
-    results = lax.all_gather(results_q, "tp", axis=1, tiled=True)
+    results = jnp.concatenate(
+        lax.all_to_all(jnp.stack([results_q] * lax.axis_size("tp")), "tp", 0, 0), axis=1
+    )
     picked = results.reshape(-1, model_width)[assign_slot].reshape(tok_rows, topk, model_width)
     moe_out = jnp.sum(expert_weights[:, :, None] * picked.astype(jnp.float32), axis=1)
     return (resid.astype(jnp.float32) + moe_out).astype(jnp.bfloat16)

time: 615 us -> 596 us (0.969)
  other arithmetic: 82.4 us -> 56.4 us
  waiting for transfers between devices: 314 us -> 299 us
  local copies, waits for them, and re-layouts: 68.3 us -> 82.5 us
  starting transfers between devices: 6.6 us -> 14.9 us
    all_gather x1 -> x0, waiting for transfers between devices: 63.5 us -> none  [shards(): results = lax.all_gather(results_q, 'tp', axis=1, tiled=True)]
    all_to_all x0 -> x1, waiting for transfers between devices: none -> 48.5 us  [shards(): lax.all_to_all(jnp.stack([results_q] * lax.axis_size('tp')), 'tp', 0, 0)]
    all_gather x1 -> x0, other arithmetic: 26.1 us -> none  [shards(): results = lax.all_gather(results_q, 'tp', axis=1, tiled=True)]
    another operation x0 -> x2, local copies, waits for them, and re-layouts: none -> 10 us  [the longest x1 7.59 us: shards(): results.reshape(-1, model_width)[assign_slot]]
    all_to_all x0 -> x1, starting transfers between devices: none -> 8.31 us  [shards(): lax.all_to_all(jnp.stack([results_q] * lax.axis_size('tp')), 'tp', 0, 0)]
    unnamed x26 -> x27, local copies, waits for them, and re-layouts: 9.89 us -> 14 us
where the time goes in v1:
time: 596 us; the launch traced here: 587 us
  waiting for transfers between devices  299 us (50%)
  blocking collectives  96.4 us (16%)
  local copies, waits for them, and re-layouts  82.5 us (14%)
  other arithmetic  56.4 us (9%)
  matrix products  23.4 us (4%)
  starting transfers between devices  14.9 us (2%)
  between operations  14.4 us (2%)
    all_to_all x1, waiting for transfers between devices, shards(): lax.all_to_all(served, 'req', split_axis=0, concat_axis=0, tiled=True)  82.7 us
    all_gather x1, waiting for transfers between devices, shards(): expert_in = lax.all_gather(expert_q, 'tp', axis=1, tiled=True)  63.4 us
    reduce_scatter x1, waiting for transfers between devices, shards(): lax.psum_scatter(partial, 'tp', scatter_dimension=1, tiled=True)  55.6 us
    psum x1, waiting for transfers between devices, shards(): lax.psum(jnp.dot(context, w_out, preferred_element_type=jnp.float32), 'tp')  48.8 us
    all_to_all x1, waiting for transfers between devices, shards(): lax.all_to_all(jnp.stack([results_q] * lax.axis_size('tp')), 'tp', 0, 0)  48.5 us
    all_to_all x1, blocking collectives, shards(): lax.all_to_all(expert_share, 'req', split_axis=0, concat_axis=0, tiled=True)  37 us
    all_to_all x1, blocking collectives, shards(): lax.all_to_all(outgoing, 'req', split_axis=0, concat_axis=0, tiled=True)  36.8 us
    all_gather x1, other arithmetic, shards(): expert_in = lax.all_gather(expert_q, 'tp', axis=1, tiled=True)  26.1 us
  transfers between devices with their start and end apart: 5, of which 5 were waited for; matrix products, arithmetic and copies ran while one was open for 2% of the time, Pallas kernels for 0%

profile of v1, /device:TPU:1, one launch (start us, length us, event | category | flops | bytes accessed | tf_op | source)
XLA Modules:
  0.0 586.9 jit_solution(15287893992253916414)
XLA Ops:
  8.4 22.6 %all_to_all.44 = s32[64,1,1]{2,1,0:T(1,128)S(1)} all-to-all(s32[64,1,1]{2,1,0:T(1,128)S(1)} %copy.65), channel_id=1, replica_groups=mesh['req'=64,'tp'=4] {'req'}, dimensions={0} | all-to-all | bytes 512 | tf_op jit(solution)/shard_map/all_to_all | solution.py:113
  32.2 4.0 gather_fusion
  36.2 5.8 all-to-all-start.1
  43.5 2.1 fusion.41
  48.4 2.1 broadcast_and_fusion
  50.6 82.7 %all-to-all-done.1 = bf16[64,1,1,128,256]{4,3,2,1,0:T(8,128)(2,1)} async-done(((bf16[64,1,1,128,256]{4,3,2,1,0:T(8,128)(2,1)}), bf16[64,1,1,128,256]{4,3,2,1,0:T(8,128)(2,1)}, u32[]{:S(2)}, u32[]{:S(2)}) %all-to-all-start.1) | async-done | bytes 4194336 | tf_op jit(solution)/shard_map/all_to_all | solution.py:117
  133.3 4.2 gather_fusion.1
  149.0 48.8 %all-reduce.2.cloned.1.call-done = f32[128,2048]{1,0:T(8,128)} async-done(((f32[128,2048]{1,0:T(8,128)}), f32[128,2048]{1,0:T(8,128)}) %all-reduce.2.cloned.1.call-update) | async-done | bytes 1048592 | tf_op jit(solution)/shard_map/psum | solution.py:145
  199.8 1.8 copy.78
  201.6 6.2 %all_to_all.38 = bf16[64,1,8192]{2,1,0:T(2,128)(2,1)S(1)} reshape(bf16[64,4,2048]{2,1,0:T(4,128)(2,1)} %copy.78) | data formatting | bytes 2097152 | tf_op jit(solution)/shard_map/all_to_all | solution.py:170
  208.3 8.1 %reduce.10 = bf16[64,8192]{1,0:T(8,128)(2,1)} reduce(bf16[64,1,8192]{2,1,0:T(2,128)(2,1)S(1)} %all_to_all.38, bf16[]{:T(256)} %broadcast.486), dimensions={1}, to_apply=%all_to_all.38.reduce_sub_computation | reduce | bytes 2097154 | tf_op jit(solution)/shard_map/all_to_all | solution.py:170
  216.5 1.8 reshape.700
  218.3 36.8 %all_to_all.45 = bf16[64,2,4096]{2,1,0:T(2,128)(2,1)S(1)} all-to-all(bf16[64,2,4096]{2,1,0:T(2,128)(2,1)S(1)} %reshape.700), channel_id=1, replica_groups=mesh['req'=64,'tp'=4] {'req'}, dimensions={0} | all-to-all | bytes 2097152 | tf_op jit(solution)/shard_map/all_to_all | solution.py:170
  255.1 3.5 reshape.701
  258.9 63.4 %all-gather.3.cloned.1.call-done = bf16[64,1,32768]{2,1,0:T(2,128)(2,1)} async-done(((bf16[64,1,8192]{2,1,0:T(2,128)(2,1)}), bf16[64,1,32768]{2,1,0:T(2,128)(2,1)}) %all-gather.3.cloned.1.call-update) | async-done | bytes 4194320 | tf_op jit(solution)/shard_map/all_gather | solution.py:171
  322.3 26.1 %reduce.6 = bf16[64,32768]{1,0:T(8,128)(2,1)} reduce(bf16[64,1,32768]{2,1,0:T(2,128)(2,1)} %all-gather.3.cloned.1.call-done, bf16[]{:T(256)} %constant.92), dimensions={1}, to_apply=%all-gather.reduce_sub_computation | reduce | bytes 8388610 | tf_op jit(solution)/shard_map/all_gather | solution.py:171
  348.4 7.4 %reshape.655 = bf16[1024,2048]{1,0:T(8,128)(2,1)} reshape(bf16[64,32768]{1,0:T(8,128)(2,1)} %reduce.6) | data formatting | bytes 8388608 | tf_op jit(solution)/shard_map/reshape | solution.py:172
  355.8 5.6 fusion.6
  361.4 9.0 %convolution_convert_fusion = bf16[1024,2048]{1,0:T(8,128)(2,1)} fusion(bf16[1,352,2048]{2,1,0:T(8,128)(2,1)S(1)} %copy-done.8, bf16[1024,2048]{1,0:T(8,128)(2,1)} %reshape.655, bf16[1,2,2048,352]{2,3,1,0:T(8,128)(2,1)} %param.20, f32[1024,352]{0,1:T(8,128)} %fusion.6), kind=kOutput, calls=%fused_computation.10 | convolution fusion | flops 2957049856 | bytes 12713984 | tf_op jit(solution)/shard_map/dot_general | solution.py:177
  370.4 7.4 %reshape.656 = bf16[64,32768]{1,0:T(8,128)(2,1)} reshape(bf16[1024,2048]{1,0:T(8,128)(2,1)} %convolution_convert_fusion) | data formatting | bytes 8388608 | tf_op jit(solution)/shard_map/reshape | solution.py:179
  377.8 55.6 %reduce-scatter.2.cloned.1.call-done = bf16[64,8192]{1,0:T(8,128)(2,1)} async-done(((bf16[64,32768]{1,0:T(8,128)(2,1)}), bf16[64,8192]{1,0:T(8,128)(2,1)}) %reduce-scatter.2.cloned.1.call-update) | async-done | bytes 1048592 | tf_op jit(solution)/shard_map/reduce_scatter | solution.py:181
  433.5 2.7 reduce.11
  436.9 37.0 %all_to_all.46 = bf16[64,2,4096]{2,1,0:T(2,128)(2,1)} all-to-all(bf16[64,2,4096]{2,1,0:T(2,128)(2,1)S(1)} %reshape.702), channel_id=1, replica_groups=mesh['req'=64,'tp'=4] {'req'}, dimensions={0} | all-to-all | bytes 2097152 | tf_op jit(solution)/shard_map/all_to_all | solution.py:182
  473.9 6.5 %reshape.703 = bf16[64,1,8192]{2,1,0:T(2,128)(2,1)S(1)} reshape(bf16[64,2,4096]{2,1,0:T(2,128)(2,1)} %all_to_all.46) | data formatting | bytes 2097152
  481.6 2.4 stack.10
  484.0 8.3 %all-to-all-start.4 = ((bf16[4,64,8192]{2,1,0:T(8,128)(2,1)}), bf16[4,64,8192]{2,1,0:T(8,128)(2,1)}, u32[]{:S(2)}, u32[]{:S(2)}) async-start(bf16[4,64,8192]{2,1,0:T(8,128)(2,1)} %stack.10), calls=%async_computation.5 | async-start | bytes 8388608 | tf_op jit(solution)/shard_map/all_to_all | solution.py:184
  492.6 48.5 %all-to-all-done.4 = bf16[4,64,8192]{2,1,0:T(8,128)(2,1)} async-done(((bf16[4,64,8192]{2,1,0:T(8,128)(2,1)}), bf16[4,64,8192]{2,1,0:T(8,128)(2,1)}, u32[]{:S(2)}, u32[]{:S(2)}) %all-to-all-start.4) | async-done | bytes 4194336 | tf_op jit(solution)/shard_map/all_to_all | solution.py:184
  541.1 7.4 %copy.81 = bf16[64,4,8192]{2,1,0:T(4,128)(2,1)} copy(bf16[64,4,8192]{2,0,1:T(8,128)(2,1)} %bitcast.37) | data formatting | bytes 8388608 | tf_op jit(solution)/shard_map/reshape | solution.py:183
  548.5 7.6 %reshape_reshape.3 = bf16[1024,2048]{1,0:T(8,128)(2,1)} reshape(bf16[64,4,8192]{2,1,0:T(4,128)(2,1)} %copy.81) | data formatting | bytes 8388608 | tf_op jit(solution)/shard_map/reshape;reshape | solution.py:186
  556.1 9.8 %gather_fusion.2 = bf16[768,2048]{1,0:T(8,128)(2,1)} fusion(bf16[1024,2048]{1,0:T(8,128)(2,1)} %reshape_reshape.3, s32[1024]{0:T(1024)S(1)} %pad_clamp_fusion), kind=kCustom, calls=%fused_computation.2 | custom fusion | bytes 6294528 | tf_op jit(solution)/shard_map/gather | solution.py:186
  565.9 6.6 %reshape.658 = f32[128,6,2048]{2,1,0:T(8,128)} reshape(bf16[768,2048]{1,0:T(8,128)(2,1)} %gather_fusion.2) | data formatting | bytes 9437184 | tf_op jit(solution)/shard_map/convert_element_type | solution.py:187
  572.5 6.8 %multiply_reduce_fusion = f32[128,2048]{1,0:T(8,128)S(1)} fusion(f32[128,6,2048]{2,1,0:T(8,128)} %reshape.658, f32[128,6]{1,0:T(8,128)S(1)} %copy.71), kind=kLoop, calls=%fused_computation.6 | loop fusion | flops 2883584 | bytes 7343104 | tf_op jit(solution)/shard_map/reduce_sum | solution.py:187
  (85 shorter events, 23.9 us)
Async XLA Ops:
  6.5 136.9 %copy-start = (bf16[512,2048]{1,0:T(8,128)(2,1)S(1)}, bf16[512,2048]{1,0:T(8,128)(2,1)}, u32[]{:S(2)}) copy-start(bf16[512,2048]{1,0:T(8,128)(2,1)} %param.18) | copy-start | bytes 6291460
  36.2 6.5 %copy-start.5 = (s32[1,128]{1,0:T(1,128)S(1)}, s32[1,128]{1,0:T(1,128)}, u32[]{:S(2)}) copy-start(s32[1,128]{1,0:T(1,128)} %param.22) | copy-start | bytes 1540
  36.2 7.1 %copy-start.2 = (bf16[128,2048]{1,0:T(8,128)(2,1)S(1)}, bf16[128,2048]{1,0:T(8,128)(2,1)}, u32[]{:S(2)}) copy-start(bf16[128,2048]{1,0:T(8,128)(2,1)} %param.14) | copy-start | bytes 1572868
  36.2 7.3 %copy-start.3 = (f32[2048]{0:T(1024)S(1)}, f32[2048]{0:T(1024)}, u32[]{:S(2)}) copy-start(f32[2048]{0:T(1024)} %param.15) | copy-start | bytes 24580
  36.2 97.1 %all-to-all-start.1 = ((bf16[64,1,1,128,256]{4,3,2,1,0:T(8,128)(2,1)}), bf16[64,1,1,128,256]{4,3,2,1,0:T(8,128)(2,1)}, u32[]{:S(2)}, u32[]{:S(2)}) async-start(bf16[64,1,1,128,256]{4,3,2,1,0:T(8,128)(2,1)} %bitcast.131), calls=%async_computation.1 | async-start | bytes 8388608 | tf_op jit(solution)/shard_map/all_to_all | solution.py:117
  42.0 3.7 copy-start.9
  42.0 155.8 %all-reduce.2.cloned.1.call-start = ((), (), s32[]{:S(2)}) async-start(), calls=%async_computation.6 | async-start | bytes 2097152 | tf_op jit(solution)/shard_map/psum | solution.py:145
  143.4 2.1 copy-start.6
  144.9 54.3 %copy-start.4 = (f32[2048]{0:T(1024)S(1)}, f32[2048]{0:T(1024)}, u32[]{:S(2)}) copy-start(f32[2048]{0:T(1024)} %param.19) | copy-start | bytes 24580
  145.0 177.3 %all-gather.3.cloned.1.call-start = ((), (), s32[]{:S(2)}) async-start(), calls=%async_computation.8 | async-start | bytes 10485760 | tf_op jit(solution)/shard_map/all_gather | solution.py:171
  258.7 174.8 %reduce-scatter.2.cloned.1.call-start = ((), (), s32[]{:S(2)}) async-start(), calls=%async_computation.7 | async-start | bytes 5242880 | tf_op jit(solution)/shard_map/reduce_scatter | solution.py:181
  355.8 5.6 copy-start.8
  484.0 8.3 %copy-start.7 = (f32[128,6]{0,1:T(8,128)S(1)}, f32[128,6]{0,1:T(8,128)}, u32[]{:S(2)}) copy-start(f32[128,6]{0,1:T(8,128)} %param.27) | copy-start | bytes 9220
  484.0 57.1 %all-to-all-start.4 = ((bf16[4,64,8192]{2,1,0:T(8,128)(2,1)}), bf16[4,64,8192]{2,1,0:T(8,128)(2,1)}, u32[]{:S(2)}, u32[]{:S(2)}) async-start(bf16[4,64,8192]{2,1,0:T(8,128)(2,1)} %stack.10), calls=%async_computation.5 | async-start | bytes 8388608 | tf_op jit(solution)/shard_map/all_to_all | solution.py:184
  572.5 7.7 %copy-start.1 = (bf16[512,2048]{1,0:T(8,128)(2,1)S(1)}, bf16[512,2048]{1,0:T(8,128)(2,1)}, u32[]{:S(2)}) copy-start(bf16[512,2048]{1,0:T(8,128)(2,1)} %param.18) | copy-start | bytes 6291460
Sparse Core Ops, SparseCore 0:
  145.1 52.6 all-reduce.1
  258.8 63.4 all-gather.2
  377.9 55.4 reduce-scatter.1
